TPU v7x, 256 devices: a whole 4x4x8 slice. The times are simulated.
256 devices in a mesh: walker: 2 (over core), grp: 128 (over z, x, y).
Axes of the slice: x: 4, y: 4, z: 8, core: 2. Of those that a mesh axis runs over, the one named last changes fastest.
Arguments:
- feats: bfloat16 [4096, 256], P(('walker', 'grp')), parts along dimension 0, may hold values from -6 to 6
- perm: int32 [4096], P('walker'), parts along dimension 0, may hold values from 0 to 2047, each once
- w_left: bfloat16 [256, 256], replicated, may hold values from -0.375 to 0.375
- w_right: bfloat16 [256, 256], replicated, may hold values from -0.375 to 0.375
- bias_in: float32 [256], replicated, may hold values from -3 to 3
- w_hidden: bfloat16 [256, 256], replicated, may hold values from -0.375 to 0.375
- bias_hidden: float32 [256], replicated, may hold values from -3 to 3
- w_out: float32 [256], replicated, may hold values from -0.375 to 0.375
- pair_strength: float32 [128], replicated, may hold values from 16 to 32
Outputs:
- log_pivot: float32 [256], P('walker'), parts along dimension 0
- panel_cols: float32 [3584, 256], P(('walker', 'grp')), parts along dimension 0
- schur: float32 [3584, 1792], P(('walker', 'grp')), parts along dimension 0
There are 2 independent parts, one for each index of `walker`. A program takes and returns all parts, laid end to end along the dimension named above; an argument that names none is the same for every part. Nothing has to cross between parts.
Inputs may be any that keep to these rules, and one draw needn't show every extreme that they name: `perm`: each position 0 to 2047 appears exactly once.
All inputs are finite; a program needn't handle non-finite values.
Results may differ from a plain program's by a relative error of at most 0.0062.
Values may be sent and summed in bfloat16 or wider, within the bound.
No kernel may reach another device: no remote copies, remote signals or barrier semaphores. Data moves between devices by JAX's collectives and lax.ppermute only.
A program may use at most 64 MiB of HBM per device.

v0:
```python
import jax
import jax.numpy as jnp
from jax import lax
from jax.sharding import PartitionSpec as P


def orbitals(left_part, right_part, bias_in, w_hidden, bias_hidden, w_out):
    pre = (
        left_part.astype(jnp.float32)[:, None, :]
        + right_part.astype(jnp.float32)[None, :, :]
        + bias_in
    )
    gated = jax.nn.silu(pre).astype(jnp.bfloat16).reshape(-1, pre.shape[-1])
    hidden = jax.nn.silu(jnp.dot(gated, w_hidden, preferred_element_type=jnp.float32) + bias_hidden)
    values = jnp.dot(hidden, w_out, precision=lax.Precision.HIGHEST)
    return values.reshape(left_part.shape[0], right_part.shape[0])


def column_width():
    return 128


def forward_terms(left_rows, right_cols, params):
    count = right_cols.shape[0]
    width = column_width()
    pieces = right_cols.reshape(count // width, width, right_cols.shape[1])
    result = lax.map(lambda piece: orbitals(left_rows, piece, *params), pieces)
    return jnp.transpose(result, (1, 0, 2)).reshape(left_rows.shape[0], count)


def backward_terms(right_rows, left_cols, params):
    count = left_cols.shape[0]
    width = column_width()
    pieces = left_cols.reshape(count // width, width, left_cols.shape[1])
    result = lax.map(lambda piece: orbitals(piece, right_rows, *params), pieces)
    return result.reshape(count, right_rows.shape[0]).T


def factor_block(block):
    size = block.shape[0]
    position = jnp.arange(size)

    def advance(step, carry):
        matrix, lower, pivots = carry
        first = (2 * step).astype(jnp.int32)
        col_even = lax.dynamic_slice_in_dim(matrix, first, 1, 1)[:, 0]
        col_odd = lax.dynamic_slice_in_dim(matrix, first + 1, 1, 1)[:, 0]
        pivot = lax.dynamic_index_in_dim(col_odd, first, 0, keepdims=False)
        keep = position >= first
        zeros = jnp.zeros_like(col_even)
        lower_even = jnp.where(keep, col_odd / pivot, zeros)
        lower_odd = jnp.where(keep, -col_even / pivot, zeros)
        lower = lax.dynamic_update_slice(
            lower, jnp.stack([lower_even, lower_odd], axis=1), (jnp.int32(0), first)
        )
        rest = position > first + 1
        keep_even = jnp.where(rest, col_even, zeros)
        keep_odd = jnp.where(rest, col_odd, zeros)
        matrix = (
            matrix
            + (keep_odd[:, None] * keep_even[None, :] - keep_even[:, None] * keep_odd[None, :])
            / pivot
        )
        pivots = lax.dynamic_update_slice(pivots, pivot[None], (step.astype(jnp.int32),))
        return (matrix, lower, pivots)

    start = (block, jnp.zeros_like(block), jnp.zeros((size // 2,), block.dtype))
    matrix, lower, pivots = lax.fori_loop(0, size // 2, advance, start)
    return (lower, pivots)


def pair_scale(columns, pivots):
    count = columns.shape[0]
    grouped = columns.reshape(count, -1, 2)
    swapped = jnp.stack([grouped[:, :, 1], -grouped[:, :, 0]], axis=2).reshape(count, -1)
    return swapped / jnp.repeat(pivots, 2)[None, :]


def solve_rows(lower, rows):
    return jax.scipy.linalg.solve_triangular(lower, rows.T, lower=True, unit_diagonal=True).T


def on_device(feats, perm, w_left, w_right, bias_in, w_hidden, bias_hidden, w_out, pair_strength):
    groups = lax.axis_size("grp")
    device = lax.axis_index("grp")
    electrons = perm.shape[0]
    panel = 2 * pair_strength.shape[0]
    share = panel // groups
    tail = (electrons - panel) // groups
    params = (bias_in, w_hidden, bias_hidden, w_out)
    left_own = jnp.dot(feats, w_left, preferred_element_type=jnp.float32).astype(jnp.bfloat16)
    right_own = jnp.dot(feats, w_right, preferred_element_type=jnp.float32).astype(jnp.bfloat16)
    left_every, right_every = (
        lax.all_gather(left_own, "grp", axis=0, tiled=True),
        lax.all_gather(right_own, "grp", axis=0, tiled=True),
    )
    left_all = jnp.take(left_every, perm, axis=0)
    right_all = jnp.take(right_every, perm, axis=0)
    top_start = device * share
    tail_start = panel + device * tail
    left_rows = jnp.concatenate(
        [
            lax.dynamic_slice_in_dim(left_all, top_start, share, 0),
            lax.dynamic_slice_in_dim(left_all, tail_start, tail, 0),
        ],
        axis=0,
    )
    right_rows = jnp.concatenate(
        [
            lax.dynamic_slice_in_dim(right_all, top_start, share, 0),
            lax.dynamic_slice_in_dim(right_all, tail_start, tail, 0),
        ],
        axis=0,
    )
    top_rows = forward_terms(left_rows[:share], right_all[:panel], params) - backward_terms(
        right_rows[:share], left_all[:panel], params
    )
    tail_rows = forward_terms(left_rows[share:], right_all, params) - backward_terms(
        right_rows[share:], left_all, params
    )
    block_rows = lax.all_gather(top_rows, "grp", axis=0, tiled=True)
    pattern = jnp.array([[0.0, 1.0], [-1.0, 0.0]], dtype=pair_strength.dtype)
    block = block_rows + jnp.kron(jnp.diag(pair_strength), pattern)
    lower, pivots = factor_block(block)
    log_pivot = jnp.log(jnp.abs(pivots))
    below_own = tail_rows[:, :panel]
    trailing_own = tail_rows[:, panel:]
    panel_own = solve_rows(lower, below_own)
    scaled_own = pair_scale(panel_own, pivots)
    schur = trailing_own - jnp.dot(
        panel_own,
        lax.all_gather(scaled_own, "grp", axis=0, tiled=True).T,
        precision=lax.Precision.HIGHEST,
    )
    return (log_pivot, panel_own, schur)


def solution(mesh):
    return jax.shard_map(
        on_device,
        mesh=mesh,
        in_specs=(P(("walker", "grp"), None), P("walker"), P(), P(), P(), P(), P(), P(), P()),
        out_specs=(P("walker"), P(("walker", "grp"), None), P(("walker", "grp"), None)),
        check_vma=False,
    )
```

profile of v0, /device:TPU:6, one launch (start us, length us, event | category | flops | bytes accessed | tf_op | source)
XLA Modules:
  0.0 1272.6 jit_solution(9753338062024064957)
XLA Ops:
  12.1 7.3 broadcast_multiply_fusion
  19.5 13.2 %mul.191 = f32[256,256]{1,0:T(8,128)} reshape(f32[128,2,128,2]{3,2,1,0:T(8,128)} %broadcast_multiply_fusion) | data formatting | bytes 524288 | tf_op jit(solution)/shard_map/jit(kron)/mul | solution.py:123
  33.8 83.8 %all-gather.6.cloned.1.call-done = bf16[2048,256]{1,0:T(8,128)(2,1)} async-done(((bf16[16,256]{1,0:T(8,128)(2,1)}), bf16[2048,256]{1,0:T(8,128)(2,1)}) %all-gather.6.cloned.1.call-update) | async-done | bytes 1048592 | tf_op jit(solution)/shard_map/all_gather | solution.py:94
  117.5 8.0 gather_fusion
  125.5 97.7 %all-gather.8.cloned.1.call-done = bf16[2048,256]{1,0:T(8,128)(2,1)} async-done(((bf16[16,256]{1,0:T(8,128)(2,1)}), bf16[2048,256]{1,0:T(8,128)(2,1)}) %all-gather.8.cloned.1.call-update) | async-done | bytes 1048592 | tf_op jit(solution)/shard_map/all_gather | solution.py:95
  223.2 8.0 gather_fusion.1
  234.8 64.1 %while.65 = (s32[]{:T(128)}, f32[16,14,128]{2,1,0:T(8,128)S(1)}, bf16[14,256]{1,0:T(8,128)(2,1)S(1)}, bf16[16,128,256]{2,1,0:T(8,128)(2,1)}, f32[256]{0:T(256)S(...) while((s32[]{:T(128)}, f32[16,14,128]{2,1,0:T(8,128)S(1)}, ...), condition=%wide.region_7.9_spmd, body=%wide.region_6.8_spmd.sunk | while | flops 245927424 | bytes 9696365 | solution.py:27
  240.8 2.0 fusion.106
  299.6 2.5 while.64
  302.2 315.5 %all-gather = f32[128,2,256]{2,1,0:T(2,128)S(1)} all-gather(f32[1,2,256]{2,1,0:T(2,128)S(1)} %fusion.53), channel_id=1, replica_groups=mesh['walker'=2,'grp'=128] {'grp'}, dimensions={0}, use_global_device_ids=true | all-gather | bytes 264192 | tf_op jit(solution)/shard_map/all_gather | solution.py:121
  618.5 107.8 %while.66 = (s32[]{:T(128)}, f32[16,128,14]{2,1,0:T(8,128)}, bf16[16,128,256]{2,1,0:T(8,128)(2,1)S(1)}, bf16[14,256]{1,0:T(8,128)(2,1)S(1)}, f32[256]{0:T(256)S(...) while((s32[]{:T(128)}, f32[16,128,14]{2,1,0:T(8,128)}, ...), condition=%wide.region_9.11_spmd, body=%wide.region_8.10_spmd.sunk | while | flops 245927424 | bytes 11606153 | solution.py:35
  620.3 2.1 convolution_add_fusion.11
  622.5 2.0 fusion.110
  627.1 2.1 convolution_add_fusion.11
  629.2 2.0 fusion.110
  633.8 2.1 convolution_add_fusion.11
  636.0 2.0 fusion.110
  640.5 2.1 convolution_add_fusion.11
  642.7 2.0 fusion.110
  647.3 2.1 convolution_add_fusion.11
  649.4 2.0 fusion.110
  654.0 2.1 convolution_add_fusion.11
  656.2 2.0 fusion.110
  660.8 2.1 convolution_add_fusion.11
  662.9 2.0 fusion.110
  667.5 2.1 convolution_add_fusion.11
  669.7 2.0 fusion.110
  674.2 2.1 convolution_add_fusion.11
  676.4 2.0 fusion.110
  681.0 2.1 convolution_add_fusion.11
  683.1 2.0 fusion.110
  687.7 2.1 convolution_add_fusion.11
  689.9 2.0 fusion.110
  694.5 2.1 convolution_add_fusion.11
  696.6 2.0 fusion.110
  701.2 2.1 convolution_add_fusion.11
  703.3 2.0 fusion.110
  707.9 2.1 convolution_add_fusion.11
  710.1 2.0 fusion.110
  714.7 2.1 convolution_add_fusion.11
  716.8 2.0 fusion.110
  721.4 2.1 convolution_add_fusion.11
  723.6 2.0 fusion.110
  729.2 365.8 %while.68 = (s32[]{:T(128)}, f32[256,256]{0,1:T(8,128)S(1)}, f32[256,256]{0,1:T(8,128)S(1)}, f32[128]{0:T(128)S(1)}, s32[]{:T(128)}, /*index=5*/s32[]{:T(128)}, s32[]{:T(128)}, s32[]{:T(128)}, s32[]{:T(128)}, s32[]{:T(128)}) while((s32[]{:T(128)}, f32[256,256]{0,1:T(8,128)S(1)}, f32[256,256]{0,1:T(8,128)S(1)}, ...), condition=%wide.region_5.7_spmd.clone.clone, body=%wide.region_4.6_spmd.clone.clone.sunk | while | flops 331276 | bytes 548637 | solution.py:68
  1095.1 5.4 while.67
  1100.6 20.5 %custom-call.4 = f32[2,128,128]{1,2,0:T(8,128)S(1)} custom-call(f32[2,128,128]{2,1,0:T(8,128)} %get-tuple-element.340), custom_call_target="InvertDiagBlocksLowerTriangular" | custom-call | tf_op jit(solution)/shard_map/jit(_solve_triangular)/triangular_solve | solution.py:80
  1123.5 138.6 %all-gather.10.cloned.1.call-done = f32[128,14,256]{2,1,0:T(8,128)} async-done(((f32[1,14,256]{2,1,0:T(8,128)}), f32[128,14,256]{2,1,0:T(8,128)}) %all-gather.10.cloned.1.call-update) | async-done | bytes 1835024 | tf_op jit(solution)/shard_map/all_gather | solution.py:132
  1263.8 2.3 convolution_subtract_fusion
  (1519 shorter events, 484.2 us)
Async XLA Ops:
  7.2 0.9 copy-start
  7.2 110.4 %all-gather.6.cloned.1.call-start = ((), (), s32[]{:S(2)}) async-start(), calls=%async_computation | async-start | bytes 1056768 | tf_op jit(solution)/shard_map/all_gather | solution.py:94
  9.5 213.7 %all-gather.8.cloned.1.call-start = ((), (), s32[]{:S(2)}) async-start(), calls=%async_computation.1 | async-start | bytes 1056768 | tf_op jit(solution)/shard_map/all_gather | solution.py:95
  11.3 1250.9 %all-gather.10.cloned.1.call-start = ((), (), s32[]{:S(2)}) async-start(), calls=%async_computation.2 | async-start | bytes 2113536 | tf_op jit(solution)/shard_map/all_gather | solution.py:132
  19.4 14.3 %copy-start.8 = (s32[2048]{0:T(1024)S(1)}, s32[2048]{0:T(1024)}, u32[]{:S(2)}) copy-start(s32[2048]{0:T(1024)} %param.23) | copy-start | bytes 24580
  231.2 1.5 copy-start.1
  231.2 1.5 copy-start.5
  231.2 1.5 copy-start.6
  231.3 1.5 copy-start.13
  231.7 1.0 copy-start.2
  232.8 1.5 copy-start.4
  234.2 0.6 copy-start.9
  234.3 65.3 %copy-start.3 = (f32[2,128,2]{2,1,0:T(8,128)S(1)}, f32[2,128,2]{2,1,0:T(8,128)}, u32[]{:S(2)}) copy-start(f32[2,128,2]{2,1,0:T(8,128)} %custom-call.10) | copy-start | bytes 6148
  299.0 0.6 copy-start.14
  299.6 2.6 copy-start.10
  299.6 0.7 copy-start.15
  300.8 0.7 copy-start.15
  620.3 2.1 copy-start.16
  627.1 2.1 copy-start.16
  633.8 2.1 copy-start.16
  640.5 2.1 copy-start.16
  647.3 2.1 copy-start.16
  654.0 2.1 copy-start.16
  660.8 2.1 copy-start.16
  667.5 2.1 copy-start.16
  674.2 2.1 copy-start.16
  681.0 2.1 copy-start.16
  687.7 2.1 copy-start.16
  694.5 2.1 copy-start.16
  701.2 2.1 copy-start.16
  707.9 2.1 copy-start.16
  714.7 2.1 copy-start.16
  721.4 2.1 copy-start.16
  726.3 2.8 copy-start.12
  729.1 365.9 %copy-start.11 = (s32[256]{0:T(256)S(1)}, s32[256]{0:T(256)}, u32[]{:S(2)}) copy-start(s32[256]{0:T(256)} %iota_add_fusion) | copy-start | bytes 3076
  729.2 365.9 %copy-start.17 = (s32[2]{0:T(128)S(1)}, s32[2]{0:T(128)}, u32[]{:S(2)}) copy-start(s32[2]{0:T(128)} %iota_multiply_fusion) | copy-start | bytes 28
  1121.6 142.3 %copy-start.7 = (f32[14,256]{1,0:T(8,128)}, f32[14,256]{1,0:T(8,128)S(1)}, u32[]{:S(2)}) copy-start(f32[14,256]{1,0:T(8,128)S(1)} %fusion.50) | copy-start | bytes 43012
Sparse Core Ops, SparseCore 0:
  12.0 105.5 all-gather.5
  121.5 101.6 all-gather.7
  1123.1 138.9 all-gather.9
where the time goes:
time: 1280 us; the launch traced here: 1270 us
  waiting for transfers between devices  320 us (25%)
  blocking collectives  315 us (25%)
  other arithmetic  256 us (20%)
  local copies, waits for them, and re-layouts  242 us (19%)
  matrix products  113 us (9%)
  between operations  14.3 us (1%)
    all_gather x1, blocking collectives, on_device(): block_rows = lax.all_gather(top_rows, 'grp', axis=0, tiled=True)  315 us
    all_gather x1, waiting for transfers between devices, on_device(): lax.all_gather(scaled_own, 'grp', axis=0, tiled=True)  139 us
    add x128, other arithmetic, advance(): matrix + (keep_odd[:, None] * keep_even[None, :] - keep_even[:, None] * k...  104 us
    all_gather x1, waiting for transfers between devices, on_device(): lax.all_gather(right_own, 'grp', axis=0, tiled=True)  97.7 us
    dynamic_update_slice x128, local copies, waits for them, and re-layouts, advance(): lax.dynamic_update_slice(pivots, pivot[None], (step.astype(jnp.int32),))  86.2 us
    select_n x128, other arithmetic, advance(): lower_odd = jnp.where(keep, -col_even / pivot, zeros)  84.3 us
    all_gather x1, waiting for transfers between devices, on_device(): lax.all_gather(left_own, 'grp', axis=0, tiled=True)  83.8 us
    dynamic_slice x128, local copies, waits for them, and re-layouts, advance(): pivot = lax.dynamic_index_in_dim(col_odd, first, 0, keepdims=False)  75.5 us
  transfers between devices with their start and end apart: 3, of which 3 were waited for; matrix products, arithmetic and copies ran while one was open for 3% of the time, Pallas kernels for 0%

commit v1 on v0

--- a/solution.py
+++ b/solution.py
@@ -2,6 +2,7 @@
 import jax.numpy as jnp
 from jax import lax
 from jax.sharding import PartitionSpec as P
+from jax.lax import all_to_all, axis_size
 
 
 def orbitals(left_part, right_part, bias_in, w_hidden, bias_hidden, w_out):
@@ -90,8 +91,15 @@
     params = (bias_in, w_hidden, bias_hidden, w_out)
     left_own = jnp.dot(feats, w_left, preferred_element_type=jnp.float32).astype(jnp.bfloat16)
     right_own = jnp.dot(feats, w_right, preferred_element_type=jnp.float32).astype(jnp.bfloat16)
+
+    def view_set(piece_in, axis_id, along_dim):
+        return jnp.concatenate(
+            all_to_all(jnp.stack([piece_in for _ in range(axis_size(axis_id))]), axis_id, 0, 0),
+            axis=along_dim,
+        )
+
     left_every, right_every = (
-        lax.all_gather(left_own, "grp", axis=0, tiled=True),
+        view_set(left_own, "grp", 0),
         lax.all_gather(right_own, "grp", axis=0, tiled=True),
     )
     left_all = jnp.take(left_every, perm, axis=0)

time: 1280 us -> 1190 us (0.930)
  waiting for transfers between devices: 320 us -> 209 us
  starting transfers between devices: 0.12 us -> 15.5 us
  local copies, waits for them, and re-layouts: 242 us -> 255 us
    all_gather x1 -> x0, waiting for transfers between devices: 83.8 us -> none  [on_device(): lax.all_gather(left_own, 'grp', axis=0, tiled=True)]
    all_gather x1, waiting for transfers between devices: 97.7 us -> 69.9 us  [on_device(): lax.all_gather(right_own, 'grp', axis=0, tiled=True)]
    all_to_all x0 -> x1, starting transfers between devices: none -> 15.4 us  [view_set(): all_to_all(jnp.stack([piece_in for _ in range(axis_size(axis_id))]), axis...]
    add x54, other arithmetic: 21.4 us -> 7.84 us  [orbitals(): left_part.astype(jnp.float32)[:, None, :]]
    convert_element_type x36, other arithmetic: 0.31 us -> 13.7 us  [orbitals(): left_part.astype(jnp.float32)[:, None, :]]
  transfers between devices with their start and end apart: 3 -> 3, of which waited for: 3 -> 2; matrix products, arithmetic and copies ran while one was open for 3% -> 3% of each run, Pallas kernels for 0% -> 0%
where the time goes in v1:
time: 1190 us
  blocking collectives  315 us (26%)
  local copies, waits for them, and re-layouts  255 us (21%)
  other arithmetic  253 us (21%)
  waiting for transfers between devices  209 us (18%)
  matrix products  113 us (9%)
  starting transfers between devices  15.5 us (1%)
  between operations  14.5 us (1%)
  loops' own time  12.3 us (1%)
    all_gather x1, blocking collectives, on_device(): block_rows = lax.all_gather(top_rows, 'grp', axis=0, tiled=True)  315 us
    all_gather x1, waiting for transfers between devices, on_device(): lax.all_gather(scaled_own, 'grp', axis=0, tiled=True)  139 us
    add x128, other arithmetic, advance(): matrix + (keep_odd[:, None] * keep_even[None, :] - keep_even[:, None] * k...  104 us
    dynamic_update_slice x128, local copies, waits for them, and re-layouts, advance(): lax.dynamic_update_slice(pivots, pivot[None], (step.astype(jnp.int32),))  86.2 us
    select_n x128, other arithmetic, advance(): lower_odd = jnp.where(keep, -col_even / pivot, zeros)  84.3 us
    dynamic_slice x128, local copies, waits for them, and re-layouts, advance(): pivot = lax.dynamic_index_in_dim(col_odd, first, 0, keepdims=False)  75.5 us
    all_gather x1, waiting for transfers between devices, on_device(): lax.all_gather(right_own, 'grp', axis=0, tiled=True)  69.9 us
    dot_general x36, matrix products, orbitals(): values = jnp.dot(hidden, w_out, precision=lax.Precision.HIGHEST)  66.7 us
  transfers between devices with their start and end apart: 3, of which 2 were waited for; matrix products, arithmetic and copies ran while one was open for 3% of the time, Pallas kernels for 0%

profile of v1, /device:TPU:6, one launch (start us, length us, event | category | flops | bytes accessed | tf_op | source)
XLA Modules:
  0.0 1188.3 jit_solution(8840530697932588268)
XLA Ops:
  11.7 15.4 %all-to-all-start = ((bf16[128,16,256]{2,1,0:T(8,128)(2,1)}), bf16[128,16,256]{2,1,0:T(8,128)(2,1)S(1)}, u32[]{:S(2)}, u32[]{:S(2)}) async-start(bf16[128,16,256]{2,1,0:T(8,128)(2,1)} %stack.18), calls=%async_computation | async-start | bytes 2097152 | tf_op jit(solution)/shard_map/all_to_all | solution.py:97
  27.3 6.6 broadcast_multiply_fusion
  33.9 13.2 %mul.191 = f32[256,256]{1,0:T(8,128)} reshape(f32[128,2,128,2]{3,2,1,0:T(8,128)} %broadcast_multiply_fusion) | data formatting | bytes 524288 | tf_op jit(solution)/shard_map/jit(kron)/mul | solution.py:131
  48.3 69.9 %all-gather.5.cloned.1.call-done = bf16[2048,256]{1,0:T(8,128)(2,1)} async-done(((bf16[16,256]{1,0:T(8,128)(2,1)}), bf16[2048,256]{1,0:T(8,128)(2,1)}) %all-gather.5.cloned.1.call-update) | async-done | bytes 1048592 | tf_op jit(solution)/shard_map/all_gather | solution.py:103
  118.1 8.0 gather_fusion.1
  126.2 7.5 gather_fusion
  135.2 64.1 %while.65 = (s32[]{:T(128)}, f32[16,14,128]{2,1,0:T(8,128)}, bf16[14,256]{1,0:T(8,128)(2,1)S(1)}, bf16[16,128,256]{2,1,0:T(8,128)(2,1)S(1)}, f32[256]{0:T(256)S(...) while((s32[]{:T(128)}, f32[16,14,128]{2,1,0:T(8,128)}, ...), condition=%wide.region_7.9_spmd, body=%wide.region_6.8_spmd.sunk | while | flops 245927424 | bytes 9699465 | solution.py:28
  200.3 2.8 while.63
  203.1 2.5 while.64
  205.7 315.5 %all-gather = f32[128,2,256]{2,1,0:T(2,128)S(1)} all-gather(f32[1,2,256]{2,1,0:T(2,128)S(1)} %fusion.53), channel_id=1, replica_groups=mesh['walker'=2,'grp'=128] {'grp'}, dimensions={0}, use_global_device_ids=true | all-gather | bytes 264192 | tf_op jit(solution)/shard_map/all_gather | solution.py:129
  521.4 121.4 %while.66 = (s32[]{:T(128)}, f32[16,128,14]{2,1,0:T(8,128)}, bf16[16,128,256]{2,1,0:T(8,128)(2,1)}, bf16[14,256]{1,0:T(8,128)(2,1)S(1)}, f32[256]{0:T(256)S(1)},...) while((s32[]{:T(128)}, f32[16,128,14]{2,1,0:T(8,128)}, ...), condition=%wide.region_9.11_spmd, body=%wide.region_8.10_spmd.sunk | while | flops 245927424 | bytes 11606153 | solution.py:36
  524.1 2.1 convolution_add_fusion.11
  526.2 2.0 fusion.110
  531.6 2.1 convolution_add_fusion.11
  533.8 2.0 fusion.110
  539.2 2.1 convolution_add_fusion.11
  541.4 2.0 fusion.110
  546.8 2.1 convolution_add_fusion.11
  549.0 2.0 fusion.110
  554.4 2.1 convolution_add_fusion.11
  556.5 2.0 fusion.110
  562.0 2.1 convolution_add_fusion.11
  564.1 2.0 fusion.110
  569.5 2.1 convolution_add_fusion.11
  571.7 2.0 fusion.110
  577.1 2.1 convolution_add_fusion.11
  579.3 2.0 fusion.110
  584.7 2.1 convolution_add_fusion.11
  586.9 2.0 fusion.110
  592.3 2.1 convolution_add_fusion.11
  594.4 2.0 fusion.110
  599.9 2.1 convolution_add_fusion.11
  602.0 2.0 fusion.110
  607.5 2.1 convolution_add_fusion.11
  609.6 2.0 fusion.110
  615.0 2.1 convolution_add_fusion.11
  617.2 2.0 fusion.110
  622.6 2.1 convolution_add_fusion.11
  624.8 2.0 fusion.110
  630.2 2.1 convolution_add_fusion.11
  632.3 2.0 fusion.110
  637.8 2.1 convolution_add_fusion.11
  639.9 2.0 fusion.110
  644.6 365.8 %while.68 = (s32[]{:T(128)}, f32[256,256]{0,1:T(8,128)S(1)}, f32[256,256]{0,1:T(8,128)S(1)}, f32[128]{0:T(128)S(1)}, s32[]{:T(128)}, /*index=5*/s32[]{:T(128)}, s32[]{:T(128)}, s32[]{:T(128)}, s32[]{:T(128)}, s32[]{:T(128)}) while((s32[]{:T(128)}, f32[256,256]{0,1:T(8,128)S(1)}, f32[256,256]{0,1:T(8,128)S(1)}, ...), condition=%wide.region_5.7_spmd.clone.clone, body=%wide.region_4.6_spmd.clone.clone.sunk | while | flops 331276 | bytes 548637 | solution.py:69
  1010.5 5.4 while.67
  1015.9 20.5 %custom-call.4 = f32[2,128,128]{1,2,0:T(8,128)S(1)} custom-call(f32[2,128,128]{2,1,0:T(8,128)} %get-tuple-element.340), custom_call_target="InvertDiagBlocksLowerTriangular" | custom-call | tf_op jit(solution)/shard_map/jit(_solve_triangular)/triangular_solve | solution.py:81
  1038.9 138.6 %all-gather.7.cloned.1.call-done = f32[128,14,256]{2,1,0:T(8,128)} async-done(((f32[1,14,256]{2,1,0:T(8,128)}), f32[128,14,256]{2,1,0:T(8,128)}) %all-gather.7.cloned.1.call-update) | async-done | bytes 1835024 | tf_op jit(solution)/shard_map/all_gather | solution.py:140
  1179.2 2.3 convolution_subtract_fusion
  (1545 shorter events, 497.8 us)
Async XLA Ops:
  7.2 0.9 copy-start
  7.2 20.1 %copy-start.9 = (f32[2,2]{1,0:T(2,128)S(1)}, f32[2,2]{1,0:T(2,128)}, u32[]{:S(2)}) copy-start(f32[2,2]{1,0:T(2,128)} %constant.221.clone) | copy-start | bytes 52
  7.2 20.0 %copy-start.10 = (f32[128]{0:T(128)S(1)}, f32[128]{0:T(128)}, u32[]{:S(2)}) copy-start(f32[128]{0:T(128)} %param.30) | copy-start | bytes 1540
  7.2 110.9 %all-gather.5.cloned.1.call-start = ((), (), s32[]{:S(2)}) async-start(), calls=%async_computation.1 | async-start | bytes 1056768 | tf_op jit(solution)/shard_map/all_gather | solution.py:103
  11.7 114.5 %all-to-all-start = ((bf16[128,16,256]{2,1,0:T(8,128)(2,1)}), bf16[128,16,256]{2,1,0:T(8,128)(2,1)S(1)}, u32[]{:S(2)}, u32[]{:S(2)}) async-start(bf16[128,16,256]{2,1,0:T(8,128)(2,1)} %stack.18), calls=%async_computation | async-start | bytes 2097152 | tf_op jit(solution)/shard_map/all_to_all | solution.py:97
  27.1 1150.5 %all-gather.7.cloned.1.call-start = ((), (), s32[]{:S(2)}) async-start(), calls=%async_computation.2 | async-start | bytes 2113536 | tf_op jit(solution)/shard_map/all_gather | solution.py:140
  33.9 14.3 %copy-start.7 = (s32[2048]{0:T(1024)S(1)}, s32[2048]{0:T(1024)}, u32[]{:S(2)}) copy-start(s32[2048]{0:T(1024)} %param.23) | copy-start | bytes 24580
  133.7 1.5 copy-start.1
  133.7 1.5 copy-start.4
  133.7 1.5 copy-start.5
  134.2 1.0 copy-start.2
  135.9 0.7 copy-start.12
  139.9 0.7 copy-start.12
  143.9 0.7 copy-start.12
  147.9 0.7 copy-start.12
  151.9 0.7 copy-start.12
  155.9 0.7 copy-start.12
  159.9 0.7 copy-start.12
  163.9 0.7 copy-start.12
  167.9 0.7 copy-start.12
  171.9 0.7 copy-start.12
  175.9 0.7 copy-start.12
  180.0 0.7 copy-start.12
  184.0 0.7 copy-start.12
  188.0 0.7 copy-start.12
  192.0 0.7 copy-start.12
  196.0 0.7 copy-start.12
  521.4 123.0 %copy-start.3 = (f32[256,256]{1,0:T(8,128)S(1)}, f32[256,256]{1,0:T(8,128)}, u32[]{:S(2)}) copy-start(f32[256,256]{1,0:T(8,128)} %mul.191) | copy-start | bytes 786436
  524.1 2.1 copy-start.14
  531.6 2.1 copy-start.14
  539.2 2.1 copy-start.14
  546.8 2.1 copy-start.14
  554.4 2.1 copy-start.14
  562.0 2.1 copy-start.14
  569.5 2.1 copy-start.14
  577.1 2.1 copy-start.14
  584.7 2.1 copy-start.14
  592.3 2.1 copy-start.14
  599.9 2.1 copy-start.14
  607.5 2.1 copy-start.14
  615.0 2.1 copy-start.14
  622.6 2.1 copy-start.14
  630.2 2.1 copy-start.14
  637.8 2.1 copy-start.14
  642.7 1.8 copy-start.11
  644.5 365.9 %copy-start.8 = (s32[256]{0:T(256)S(1)}, s32[256]{0:T(256)}, u32[]{:S(2)}) copy-start(s32[256]{0:T(256)} %iota_add_fusion) | copy-start | bytes 3076
  644.5 365.9 %copy-start.15 = (s32[2]{0:T(128)S(1)}, s32[2]{0:T(128)}, u32[]{:S(2)}) copy-start(s32[2]{0:T(128)} %iota_multiply_fusion) | copy-start | bytes 28
  1036.9 142.3 %copy-start.6 = (f32[14,256]{1,0:T(8,128)}, f32[14,256]{1,0:T(8,128)S(1)}, u32[]{:S(2)}) copy-start(f32[14,256]{1,0:T(8,128)S(1)} %fusion.50) | copy-start | bytes 43012
  (2 other events, 1.4 us)
Sparse Core Ops, SparseCore 0:
  12.0 106.1 all-gather.4
  1038.5 138.9 all-gather.6
